TPU v7x, 32 devices: a whole 2x2x4 slice. The times are simulated.
32 devices in a mesh: seq: 8 (over y, x, core), head: 4 (over z).
Axes of the slice: x: 2, y: 2, z: 4, core: 2. Of those that a mesh axis runs over, the one named last changes fastest.
Arguments:
- tokens: bfloat16 [8192, 1024], P(('seq', 'head')), may hold values from -6 to 6
- qkv_weight: bfloat16 [1024, 3, 1024], P(None, None, 'head'), may hold values from -0.1875 to 0.1875
- out_weight: bfloat16 [1024, 1024], P('head'), may hold values from -0.1875 to 0.1875
- up_weight: bfloat16 [1024, 2, 2816], P(None, None, 'head'), may hold values from -0.1875 to 0.1875
- down_weight: bfloat16 [2816, 1024], P('head'), may hold values from -0.109375 to 0.109375
- vocab_weight: bfloat16 [1024, 16384], P(None, 'head'), may hold values from -0.1875 to 0.1875
- persistent: bfloat16 [2, 16, 1024], P(None, None, 'head'), may hold values from -120 to 120
- norm_gains: float32 [3, 1024], replicated, may hold values from 0.5 to 1.5
- write_rate: float32 [8192, 8], P('seq', 'head'), may hold values from 0.02 to 0.2
- forget: float32 [128, 8], P('seq', 'head'), may hold values from 0 to 1
- momentum: float32 [128, 8], P('seq', 'head'), may hold values from 0.2 to 0.9
- prompt_spans: int32 [4], replicated, may hold values from 1 to 64, as said below
Outputs:
- logit_max: float32 [8192], P('seq')
- state_rms: float32 [4, 8], P(None, 'head')
Inputs may be any that keep to these rules, and one draw needn't show every extreme that they name: Prompt p holds prompt_spans[p] consecutive spans of 64 tokens, the prompts packed in order from token 0; they sum to 128, and prompt 1 is the longest, with exactly 64 spans.
All inputs are finite; a program needn't handle non-finite values.
Results may differ from a plain program's by a relative error of at most 0.0047.
Values may be sent and summed in bfloat16 or wider, within the bound.
No kernel may reach another device: no remote copies, remote signals or barrier semaphores. Data moves between devices by JAX's collectives and lax.ppermute only.
A program may use at most 128 MiB of HBM per device.

v0:
```python
import jax
import jax.numpy as jnp
from jax import lax
from jax.sharding import PartitionSpec as P

D = 1024
HS = 128
NPER = 16
SEG = 1024
CH = 64
SEQS = 4
eps_norm = 1e-05
eps_unit = 1e-06
score_scale = 10.0
masked_score = -1e30


def passed_along(array, axis, by):
    size = lax.axis_size(axis)
    pairs = [(i, i + by) for i in range(size) if 0 <= i + by < size]
    return lax.ppermute(array, axis, pairs)


def carried_in(part, axis, combine, identity):
    place = lax.axis_index(axis)
    gathered = jax.tree.map(lambda a: lax.all_gather(a, axis), part)
    state = jax.tree.map(lambda a, e: jnp.zeros_like(a) + jnp.asarray(e, a.dtype), part, identity)

    def one(step, state):
        return combine(
            state, jax.tree.map(lambda a: lax.dynamic_index_in_dim(a, step, 0, False), gathered)
        )

    return lax.fori_loop(0, place, one, state)


def rms_scale(values, gain):
    return values * lax.rsqrt(jnp.mean(values * values, axis=-1, keepdims=True) + eps_norm) * gain


def unit_rows(values):
    widened = values.astype(jnp.float32)
    return (
        widened * lax.rsqrt(jnp.sum(widened * widened, axis=-1, keepdims=True) + eps_unit)
    ).astype(jnp.bfloat16)


def segment_starts(positions, prompt_spans):
    prompt_ends = jnp.cumsum(prompt_spans)
    first_tokens = (prompt_ends - prompt_spans) * CH
    reached = positions[:, None] >= first_tokens[None, :]
    prompt_first = jnp.max(jnp.where(reached, first_tokens[None, :], 0), axis=1)
    return prompt_first + (positions - prompt_first) // SEG * SEG


def compose(later, earlier):
    return jnp.stack(
        [
            later[..., 0] * earlier[..., 0],
            later[..., 0] * earlier[..., 1] + later[..., 1] * earlier[..., 2],
            later[..., 2] * earlier[..., 2],
        ],
        axis=-1,
    )


def apply_map(coeffs, memory, moment):
    moved_memory = coeffs[:, 0, None, None] * memory + coeffs[:, 1, None, None] * moment
    return (moved_memory, coeffs[:, 2, None, None] * moment)


def chain_combine(earlier, later):
    moved_memory, moved_moment = apply_map(later[0], earlier[1], earlier[2])
    return (compose(later[0], earlier[0]), moved_memory + later[1], moved_moment + later[2])


def to_owners(local_rows, project):
    return project(lax.all_gather(local_rows, "head", axis=0, tiled=True), jnp.int32(0))


def from_owners(term, share_rows):
    return lax.psum_scatter(
        term(jnp.int32(0), share_rows * lax.axis_size("head")),
        "head",
        scatter_dimension=0,
        tiled=True,
    )


def local(
    tokens,
    qkv_weight,
    out_weight,
    up_weight,
    down_weight,
    vocab_weight,
    persistent,
    norm_gains,
    write_rate,
    forget,
    momentum,
    prompt_spans,
):
    share_rows = tokens.shape[0]
    head_count = lax.axis_size("head")
    seq_count = lax.axis_size("seq")
    block_rows = share_rows * head_count
    heads_here = write_rate.shape[1]
    current_width = heads_here * HS
    seq_index = lax.axis_index("seq")
    head_index = lax.axis_index("head")
    qkv_matrix = qkv_weight.reshape(D, 3 * current_width)
    highest = lax.Precision.HIGHEST

    def token_project(piece, start):
        normed = rms_scale(piece.astype(jnp.float32), norm_gains[0]).astype(jnp.bfloat16)
        projected = jnp.dot(normed, qkv_matrix, preferred_element_type=jnp.float32).astype(
            jnp.bfloat16
        )
        return projected

    gathered = to_owners(tokens, token_project)
    projected = gathered
    query_unit = unit_rows(projected[:, :current_width].reshape(block_rows, heads_here, HS))
    key_unit = unit_rows(
        projected[:, current_width : 2 * current_width].reshape(block_rows, heads_here, HS)
    )
    value_rows = projected[:, 2 * current_width :].reshape(block_rows, heads_here, HS)
    reach = SEG // block_rows
    moved_keys, moved_values = passed_along((key_unit, value_rows), "seq", 1)
    earlier_keys = [moved_keys]
    earlier_values = [moved_values]
    all_keys = jnp.concatenate(earlier_keys + [key_unit], axis=0)
    all_values = jnp.concatenate(earlier_values + [value_rows], axis=0)
    first_row = seq_index * block_rows
    query_positions = first_row + jnp.arange(block_rows, dtype=jnp.int32)
    key_positions = (
        first_row - reach * block_rows + jnp.arange((reach + 1) * block_rows, dtype=jnp.int32)
    )
    query_segments = segment_starts(query_positions, prompt_spans)
    key_segments = segment_starts(key_positions, prompt_spans)
    allowed = (
        (key_segments[None, :] == query_segments[:, None])
        & (key_positions[None, :] <= query_positions[:, None])
        & (key_positions[None, :] >= 0)
    )
    persist_keys = persistent[0].reshape(NPER, heads_here, HS)
    persist_values = persistent[1].reshape(NPER, heads_here, HS)
    scores = score_scale * jnp.einsum(
        "qhd,khd->hqk", query_unit, all_keys, preferred_element_type=jnp.float32
    )
    scores = jnp.where(allowed[None], scores, masked_score)
    extra = score_scale * jnp.einsum(
        "qhd,phd->hqp", query_unit, persist_keys, preferred_element_type=jnp.float32
    )
    top = jnp.maximum(jnp.max(scores, axis=-1), jnp.max(extra, axis=-1))[..., None]
    near = jnp.where(allowed[None], jnp.exp(scores - top), 0.0)
    far = jnp.exp(extra - top)
    total = jnp.sum(near, axis=-1, keepdims=True) + jnp.sum(far, axis=-1, keepdims=True)
    near_weights = (near / total).astype(jnp.bfloat16)
    far_weights = (far / total).astype(jnp.bfloat16)
    attended = jnp.einsum(
        "hqk,khd->qhd", near_weights, all_values, preferred_element_type=jnp.float32
    )
    attended = attended + jnp.einsum(
        "hqp,phd->qhd", far_weights, persist_values, preferred_element_type=jnp.float32
    )
    total_spans = block_rows // CH
    span_queries = query_unit.reshape(total_spans, CH, heads_here, HS)
    span_keys = key_unit.reshape(total_spans, CH, heads_here, HS)
    span_values = value_rows.reshape(total_spans, CH, heads_here, HS)
    span_rates = write_rate.reshape(total_spans, CH, heads_here)
    prompt_ends = jnp.cumsum(prompt_spans)
    first_spans = prompt_ends - prompt_spans
    span_ids = seq_index * total_spans + jnp.arange(total_spans, dtype=jnp.int32)
    keep = jnp.where(jnp.any(span_ids[:, None] == first_spans[None, :], axis=1), 0.0, 1.0).astype(
        jnp.float32
    )
    causal = (jnp.arange(CH)[:, None] >= jnp.arange(CH)[None, :]).astype(jnp.float32)
    values_wide = span_values.astype(jnp.float32)
    written = jnp.einsum(
        "cthi,cthj->chij",
        span_rates[..., None] * values_wide,
        span_keys.astype(jnp.float32),
        precision=highest,
    )
    affinity = jnp.einsum(
        "cthd,cshd->chts", span_queries, span_keys, preferred_element_type=jnp.float32
    )
    affinity = affinity * causal[None, None] * jnp.transpose(span_rates, (0, 2, 1))[:, :, None, :]
    local_recall = jnp.einsum("chts,cshi->cthi", affinity, values_wide, precision=highest)
    decay_memory = forget * keep[:, None]
    decay_moment = momentum * keep[:, None]
    identity_coeffs = jnp.tile(jnp.array([1.0, 0.0, 1.0], jnp.float32), (heads_here, 1))
    zero_state = jnp.zeros((heads_here, HS, HS), jnp.float32)

    def advance(carry, inputs):
        coeffs, memory, moment = carry
        current_written, memory_rate, moment_rate = inputs
        step_coeffs = jnp.stack([memory_rate, moment_rate, moment_rate], axis=-1)
        next_moment = moment_rate[:, None, None] * moment + current_written
        next_memory = (
            memory_rate[:, None, None] * memory
            + moment_rate[:, None, None] * moment
            + current_written
        )
        return ((compose(step_coeffs, coeffs), next_memory, next_moment), (coeffs, memory))

    (last_coeffs, last_memory, last_moment), (coeffs_before, memory_before) = lax.scan(
        advance, (identity_coeffs, zero_state, zero_state), (written, decay_memory, decay_moment)
    )
    _, incoming_memory, incoming_moment = carried_in(
        (last_coeffs, last_memory, last_moment),
        "seq",
        chain_combine,
        (identity_coeffs, zero_state, zero_state),
    )
    true_before = (
        memory_before
        + coeffs_before[..., 0, None, None] * incoming_memory[None]
        + coeffs_before[..., 1, None, None] * incoming_moment[None]
    )
    recalled = local_recall + jnp.einsum(
        "chij,cthj->cthi",
        true_before * keep[:, None, None, None],
        span_queries.astype(jnp.float32),
        precision=highest,
    )
    memory_after = jnp.concatenate([memory_before[1:], last_memory[None]], axis=0)
    coeffs_after = jnp.concatenate([coeffs_before[1:], last_coeffs[None]], axis=0)
    true_after = (
        memory_after
        + coeffs_after[..., 0, None, None] * incoming_memory[None]
        + coeffs_after[..., 1, None, None] * incoming_moment[None]
    )
    spread = jnp.sqrt(jnp.mean(true_after * true_after, axis=(2, 3)))
    hit_spans = span_ids[None, :] == (prompt_ends - 1)[:, None]
    state_slots = jnp.sum(jnp.where(hit_spans[:, :, None], spread[None], 0.0), axis=1)
    mixed = (
        (attended + recalled.reshape(block_rows, heads_here, HS))
        .astype(jnp.bfloat16)
        .reshape(block_rows, current_width)
    )
    ff_here = down_weight.shape[0]
    gate_up = up_weight.reshape(D, 2 * ff_here)

    def ffn_hidden(normed_rows):
        gated = jnp.dot(normed_rows, gate_up, preferred_element_type=jnp.float32)
        return (jax.nn.silu(gated[:, :ff_here]) * gated[:, ff_here:]).astype(jnp.bfloat16)

    def ffn_project(piece, start):
        return ffn_hidden(piece)

    def attn_term(start, count):
        return jnp.dot(mixed, out_weight, preferred_element_type=jnp.float32)

    residual = tokens.astype(jnp.float32) + from_owners(attn_term, share_rows)
    hidden = to_owners(rms_scale(residual, norm_gains[1]).astype(jnp.bfloat16), ffn_project)

    def down_term(start, count):
        return jnp.dot(hidden, down_weight, preferred_element_type=jnp.float32)

    second = residual + from_owners(down_term, share_rows)
    final = rms_scale(second, norm_gains[2]).astype(jnp.bfloat16)

    def vocab_maxima(piece, start):
        return jnp.max(jnp.dot(piece, vocab_weight, preferred_element_type=jnp.float32), axis=1)

    row_maxima = to_owners(final, vocab_maxima)
    token_total = block_rows * seq_count
    logit_full = lax.dynamic_update_slice(
        jnp.full((token_total,), masked_score, jnp.float32), row_maxima, (first_row,)
    )
    norm_full = lax.dynamic_update_slice(
        jnp.zeros((SEQS, heads_here * head_count), jnp.float32),
        state_slots,
        (0, head_index * heads_here),
    )
    logit_full, norm_full = lax.pmax((logit_full, norm_full), ("seq", "head"))
    logit_max = lax.dynamic_slice(logit_full, (first_row,), (block_rows,))
    state_rms = lax.dynamic_slice(norm_full, (0, head_index * heads_here), (SEQS, heads_here))
    return (logit_max, state_rms)


def solution(mesh):
    in_specs = (
        P(("seq", "head"), None),
        P(None, None, "head"),
        P("head", None),
        P(None, None, "head"),
        P("head", None),
        P(None, "head"),
        P(None, None, "head"),
        P(),
        P("seq", "head"),
        P("seq", "head"),
        P("seq", "head"),
        P(),
    )
    out_specs = (P("seq"), P(None, "head"))
    return jax.shard_map(local, mesh=mesh, in_specs=in_specs, out_specs=out_specs, check_vma=False)
```

profile of v0, /device:TPU:0, one launch (start us, length us, event | category | flops | bytes accessed | tf_op | source)
XLA Modules:
  0.0 530.5 jit_solution(4990581086919574727)
XLA Ops:
  12.3 2.6 copy.195
  16.5 41.8 %all-gather.10.cloned.1.call-done = bf16[1024,1024]{1,0:T(8,128)(2,1)} async-done(((bf16[256,1024]{1,0:T(8,128)(2,1)}), bf16[1024,1024]{1,0:T(8,128)(2,1)}) %all-gather.10.cloned.1.call-update) | async-done | bytes 2097168 | tf_op jit(solution)/shard_map/all_gather | solution.py:78
  60.5 3.3 fusion.23
  69.8 2.8 reshape.345
  72.7 3.5 copy.206
  76.2 3.1 convert_multiply_fusion.2
  79.2 3.5 fusion.44
  82.8 29.3 %while.34 = (s32[]{:T(128)}, f32[2,3]{0,1:T(4,128)S(1)}, f32[2,128,128]{2,1,0:T(8,128)S(1)}, f32[2,128,128]{2,1,0:T(8,128)S(1)}, f32[16,2,3]{2,1,0:T(2,128)S(1)}...) while((s32[]{:T(128)}, f32[2,3]{0,1:T(4,128)S(1)}, ...), condition=%wide.region_12.13_spmd.clone, body=%wide.region_11.12_spmd.clone.sunk | while | flops 262167 | bytes 919908 | solution.py:209
  114.2 6.5 %and_and_fusion = pred[1024,2048]{1,0:T(8,128)(4,1)} fusion(s32[2048]{0:T(1024)S(1)} %iota_add_fusion, s32[2048]{0:T(1024)S(1)} %fusion.59, s32[1024]{0:T(1024)S(1)} %iota_add_fusion.1, s32[1024]{0:T(1024)S(1)} %fusion.66, pred[2048]{0:T(1024)(128)(4,1)S(1)} %fusion.63), kind=kLoop, calls=%fused_computation.25 | loop fusion | flops 8388608 | bytes 2123776 | tf_op jit(solution)/shard_map/and | solution.py:143
  123.1 2.6 copy.196
  125.7 2.6 copy.197
  129.8 3.7 collective-permute-start.1
  133.6 9.5 %all-gather.3 = f32[8,2,3]{2,1,0:T(2,128)} all-gather(f32[1,2,3]{2,1,0:T(2,128)S(1)} %bitcast.116), channel_id=2, replica_groups=mesh['seq'=8,'head'=4] {'seq'}, dimensions={0}, use_global_device_ids=true | all-gather | bytes 216 | tf_op jit(solution)/shard_map/all_gather | solution.py:26
  143.1 2.8 reshape.344
  146.1 3.5 copy.203
  153.2 3.3 fusion.32
  156.5 5.0 fusion.3
  161.5 5.6 %fusion.4 = f32[2,1024]{1,0:T(2,128)S(1)} fusion(f32[2,1024,2048]{2,1,0:T(8,128)S(1)} %get-tuple-element.215, f32[2,1024]{1,0:T(2,128)S(1)} %max.11, pred[1024,2048]{1,0:T(8,128)(4,1)S(1)} %copy-done.10), kind=kLoop, calls=%fused_computation.24 | loop fusion | flops 20969472 | bytes 18890752 | tf_op jit(solution)/shard_map/reduce_sum | solution.py:159
  168.5 4.2 all-gather.16.cloned.1.call-done
  173.5 4.3 fusion.29
  179.6 2.5 copy.219
  182.1 10.5 %fusion.36 = bf16[1024,2,128]{0,2,1:T(8,128)(2,1)S(1)} fusion(f32[1024,2,128]{0,2,1:T(8,128)} %copy.219, f32[1024,2,128]{0,2,1:T(8,128)} %convolution_bitcast_fusion, f32[2,1024,2048]{2,1,0:T(8,128)} %copy-done.5, f32[2,1024]{1,0:T(2,128)S(1)} %add.226, f32[2,1024]{1,0:T(2,128)S(1)} %max.11, pred[1024,2048]{1,0:T(8,128)(4,1)} %and_and_fusion, ...), kind=kOutput, calls=%fused_computation.59 | convolution fusion | flops 1101791232 | bytes 22560768 | tf_op jit(solution)/shard_map/hqk,khd->qhd/dot_general | solution.py:162
  192.6 2.7 fusion.79
  195.4 90.1 %reduce-scatter.3.cloned.1.call-done = f32[256,1024]{1,0:T(8,128)} async-done(((f32[1024,1024]{1,0:T(8,128)}), f32[256,1024]{1,0:T(8,128)}) %reduce-scatter.3.cloned.1.call-update) | async-done | bytes 1048592 | tf_op jit(solution)/shard_map/reduce_scatter | solution.py:82
  288.1 46.6 %all-gather.12.cloned.1.call-done = bf16[1024,1024]{1,0:T(8,128)(2,1)} async-done(((bf16[256,1024]{1,0:T(8,128)(2,1)}), bf16[1024,1024]{1,0:T(8,128)(2,1)}) %all-gather.12.cloned.1.call-update) | async-done | bytes 2097168 | tf_op jit(solution)/shard_map/all_gather | solution.py:78
  334.7 5.2 fusion.80
  339.9 3.8 fusion.26
  344.0 75.4 %reduce-scatter.5.cloned.1.call-done = f32[256,1024]{1,0:T(8,128)} async-done(((f32[1024,1024]{1,0:T(8,128)}), f32[256,1024]{1,0:T(8,128)}) %reduce-scatter.5.cloned.1.call-update) | async-done | bytes 1048592 | tf_op jit(solution)/shard_map/reduce_scatter | solution.py:82
  424.9 3.0 slice.90
  430.6 39.5 %all-gather.14.cloned.1.call-done = bf16[1024,1024]{1,0:T(8,128)(2,1)} async-done(((bf16[256,1024]{1,0:T(8,128)(2,1)}), bf16[1024,1024]{1,0:T(8,128)(2,1)}) %all-gather.14.cloned.1.call-update) | async-done | bytes 2097168 | tf_op jit(solution)/shard_map/all_gather | solution.py:78
  470.1 12.9 %convolution_reduce_fusion = f32[1024]{0:T(1024)S(1)} fusion(bf16[1024,1024]{1,0:T(8,128)(2,1)} %all-gather.14.cloned.1.call-done, bf16[1024,4096]{1,0:T(8,128)(2,1)} %param.22), kind=kOutput, calls=%fused_computation.32 | convolution fusion | flops 8594127872 | bytes 10489856 | tf_op jit(solution)/shard_map/dot_general | solution.py:267
  483.3 39.0 %all-reduce = (f32[8192]{0:T(1024)S(1)}, f32[4,8]{0,1:T(8,128)S(1)}) all-reduce(f32[8192]{0:T(1024)S(1)} %dynamic_update_slice.14, f32[4,8]{0,1:T(8,128)S(1)} %constant_dynamic-update-slice_fusion.1), channel_id=1, replica_groups=mesh['seq'=8,'head'=4] {'seq','head'}, use_global_device_ids=true, to_apply=%region_20.21 | all-reduce | flops 8224 | bytes 65792 | tf_op jit(solution)/shard_map/pmax | solution.py:279
  (276 shorter events, 69.9 us)
Async XLA Ops:
  7.2 327.5 %copy-start = (bf16[1024,2,704]{0,2,1:T(8,128)(2,1)S(1)}, bf16[1024,2,704]{0,2,1:T(8,128)(2,1)}, u32[]{:S(2)}) copy-start(bf16[1024,2,704]{0,2,1:T(8,128)(2,1)} %param.20) | copy-start | bytes 8650756
  7.2 7.7 %copy-start.29 = (s32[4]{0:T(128)S(1)}, s32[4]{0:T(128)}, u32[]{:S(2)}) copy-start(s32[4]{0:T(128)} %param.28) | copy-start | bytes 52
  7.2 8.6 %copy-start.24 = (bf16[2,16,256]{2,1,0:T(8,128)(2,1)S(1)}, bf16[2,16,256]{2,1,0:T(8,128)(2,1)}, u32[]{:S(2)}) copy-start(bf16[2,16,256]{2,1,0:T(8,128)(2,1)} %param.23) | copy-start | bytes 49156
  7.2 8.6 %copy-start.25 = (f32[3,1024]{1,0:T(4,128)S(1)}, f32[3,1024]{1,0:T(4,128)}, u32[]{:S(2)}) copy-start(f32[3,1024]{1,0:T(4,128)} %param.24) | copy-start | bytes 36868
  7.2 51.1 %all-gather.10.cloned.1.call-start = ((), (), s32[]{:S(2)}) async-start(), calls=%async_computation.2 | async-start | bytes 2621440 | tf_op jit(solution)/shard_map/all_gather | solution.py:78
  7.9 160.6 %all-gather.18.cloned.1.call-start = ((), (), s32[]{:S(2)}) async-start(), calls=%async_computation.8 | async-start | bytes 1179648 | tf_op jit(solution)/shard_map/all_gather | solution.py:26
  76.2 3.1 copy-start.7
  79.2 3.5 copy-start.30
  112.2 13.5 %copy-start.1 = (f32[2,128,128]{2,1,0:T(8,128)}, f32[2,128,128]{2,1,0:T(8,128)S(1)}, u32[]{:S(2)}) copy-start(f32[2,128,128]{2,1,0:T(8,128)S(1)} %get-tuple-element.115) | copy-start | bytes 393220
  112.2 37.4 %copy-start.18 = (f32[16,2,3]{2,1,0:T(2,128)}, f32[16,2,3]{2,1,0:T(2,128)S(1)}, u32[]{:S(2)}) copy-start(f32[16,2,3]{2,1,0:T(2,128)S(1)} %get-tuple-element.113) | copy-start | bytes 1156
  112.8 59.9 %all-gather.16.cloned.1.call-start = ((), (), s32[]{:S(2)}) async-start(), calls=%async_computation.7 | async-start | bytes 1179648 | tf_op jit(solution)/shard_map/all_gather | solution.py:26
  120.6 61.5 %collective-permute-start = (bf16[1024,2,128]{0,2,1:T(8,128)(2,1)}, bf16[1024,2,128]{0,2,1:T(8,128)(2,1)}, u32[]{:S(2)}, u32[]{:S(2)}) collective-permute-start(bf16[1024,2,128]{0,2,1:T(8,128)(2,1)} %bitcast.5), channel_id=1, source_target_pairs={{0,4},{4,8},{8,12},{12,16},{16,20},{20,24},{24,28},{1,5},{5,9},{9,... | collective-permute-start | bytes 1572872 | tf_op jit(solution)/shard_map/ppermute | solution.py:21
  129.8 26.7 %collective-permute-start.1 = (bf16[1024,2,128]{2,0,1:T(8,128)(2,1)S(1)}, bf16[1024,2,128]{2,0,1:T(8,128)(2,1)}, u32[]{:S(2)}, u32[]{:S(2)}) collective-permute-start(bf16[1024,2,128]{2,0,1:T(8,128)(2,1)S(1)} %multiply_convert_fusion.4), channel_id=1, source_target_pairs={{0,4},{4,8},{8,12},{12,16},{16,20},{20,24},{24,28},{1,5},{5,9},{9,... | collective-permute-start | bytes 1572872 | tf_op jit(solution)/shard_map/ppermute | solution.py:21
  133.6 12.3 %copy-start.26 = (f32[2,3]{1,0:T(2,128)}, f32[2,3]{1,0:T(2,128)S(1)}, u32[]{:S(2)}) copy-start(f32[2,3]{1,0:T(2,128)S(1)} %copy.215) | copy-start | bytes 76
  151.2 134.3 %reduce-scatter.3.cloned.1.call-start = ((), (), s32[]{:S(2)}) async-start(), calls=%async_computation.3 | async-start | bytes 5242880 | tf_op jit(solution)/shard_map/reduce_scatter | solution.py:82
  151.3 5.2 copy-start.10
  151.3 5.2 copy-start.15
  161.4 5.7 %copy-start.5 = (f32[2,1024,2048]{2,1,0:T(8,128)}, f32[2,1024,2048]{2,1,0:T(8,128)S(1)}, u32[]{:S(2)}) copy-start(f32[2,1024,2048]{2,1,0:T(8,128)S(1)} %get-tuple-element.215) | copy-start | bytes 50331652
  161.5 5.7 %copy-start.22 = (bf16[16,2,128]{2,1,0:T(2,128)(2,1)S(1)}, bf16[16,2,128]{2,1,0:T(2,128)(2,1)}, u32[]{:S(2)}) copy-start(bf16[16,2,128]{2,1,0:T(2,128)(2,1)} %reshape_squeeze.7) | copy-start | bytes 24580
  173.0 4.8 copy-start.8
  173.5 4.3 copy-start.12
  173.5 4.3 copy-start.13
  182.1 10.5 %copy-start.17 = (bf16[256,1024]{1,0:T(8,128)(2,1)S(1)}, bf16[256,1024]{1,0:T(8,128)(2,1)}, u32[]{:S(2)}) copy-start(bf16[256,1024]{1,0:T(8,128)(2,1)} %param.19) | copy-start | bytes 1572868
  195.3 90.2 %copy-start.6 = (bf16[256,1024]{1,0:T(8,128)(2,1)S(1)}, bf16[256,1024]{1,0:T(8,128)(2,1)}, u32[]{:S(2)}) copy-start(bf16[256,1024]{1,0:T(8,128)(2,1)} %param.17) | copy-start | bytes 1572868
  195.3 91.7 %copy-start.23 = (f32[1,1024]{1,0:T(1,128)S(1)}, f32[1,1024]{1,0:T(1,128)}, u32[]{:S(2)}) copy-start(f32[1,1024]{1,0:T(1,128)} %get-tuple-element.208) | copy-start | bytes 12292
  195.3 139.4 %all-gather.12.cloned.1.call-start = ((), (), s32[]{:S(2)}) async-start(), calls=%async_computation.4 | async-start | bytes 2621440 | tf_op jit(solution)/shard_map/all_gather | solution.py:78
  288.1 131.2 %reduce-scatter.5.cloned.1.call-start = ((), (), s32[]{:S(2)}) async-start(), calls=%async_computation.5 | async-start | bytes 5242880 | tf_op jit(solution)/shard_map/reduce_scatter | solution.py:82
  334.7 5.2 copy-start.31
  343.7 126.4 %all-gather.14.cloned.1.call-start = ((), (), s32[]{:S(2)}) async-start(), calls=%async_computation.6 | async-start | bytes 2621440 | tf_op jit(solution)/shard_map/all_gather | solution.py:78
  421.3 3.5 copy-start.19
  423.2 5.0 copy-start.2
  423.2 5.0 copy-start.9
  (10 other events, 12.1 us)
Sparse Core Ops, SparseCore 0:
  9.6 48.6 all-gather.9
  113.0 23.5 all-gather.17
  151.4 21.3 all-gather.15
  195.5 89.9 reduce-scatter.2
  288.2 46.4 all-gather.11
  343.8 75.4 reduce-scatter.4
  423.4 46.6 all-gather.13
where the time goes:
time: 540 us; the launch traced here: 531 us
  waiting for transfers between devices  298 us (55%)
  other arithmetic  58.8 us (11%)
  matrix products  58.3 us (11%)
  blocking collectives  48.5 us (9%)
  local copies, waits for them, and re-layouts  44.2 us (8%)
  between operations  14.9 us (3%)
  starting transfers between devices  6.71 us (1%)
    reduce_scatter x2, waiting for transfers between devices, from_owners(): lax.psum_scatter(term(jnp.int32(0), share_rows * lax.axis_size('head')),...  165 us
    all_gather x3, waiting for transfers between devices, to_owners(): lax.all_gather(local_rows, 'head', axis=0, tiled=True)  128 us
    pmax x1, blocking collectives, local(): logit_full, norm_full = lax.pmax((logit_full, norm_full), ('seq', 'head'))  39 us
    convert_element_type x6, local copies, waits for them, and re-layouts, unit_rows(): widened = values.astype(jnp.float32)  17.8 us
    add x16, other arithmetic, advance(): next_moment = moment_rate[:, None, None] * moment + current_written  16 us
    dot_general x1, matrix products, vocab_maxima(): jnp.dot(piece, vocab_weight, preferred_element_type=jnp.float32)  12.9 us
  transfers between devices with their start and end apart: 9, of which 6 were waited for; matrix products, arithmetic and copies ran while one was open for 12% of the time, Pallas kernels for 0%

commit v1 on v0

--- a/solution.py
+++ b/solution.py
@@ -15,6 +15,18 @@
 masked_score = -1e30
 
 
+def collect(shard, axis, dim):
+    ways, here = (lax.axis_size(axis), lax.axis_index(axis))
+    grown, reach = (shard, 1)
+    while reach < ways:
+        theirs = lax.ppermute(grown, axis, [(d, d ^ reach) for d in range(ways)])
+        mine_first = jnp.concatenate([grown, theirs], axis=dim)
+        theirs_first = jnp.concatenate([theirs, grown], axis=dim)
+        grown = jnp.where(here & reach == 0, mine_first, theirs_first)
+        reach = 2 * reach
+    return grown
+
+
 def passed_along(array, axis, by):
     size = lax.axis_size(axis)
     pairs = [(i, i + by) for i in range(size) if 0 <= i + by < size]
@@ -75,7 +87,7 @@
 
 
 def to_owners(local_rows, project):
-    return project(lax.all_gather(local_rows, "head", axis=0, tiled=True), jnp.int32(0))
+    return project(collect(local_rows, "head", 0), jnp.int32(0))
 
 
 def from_owners(term, share_rows):

time: 540 us -> 599 us (1.11)
  waiting for transfers between devices: 298 us -> 332 us
  starting transfers between devices: 6.71 us -> 32.5 us
    ppermute x0 -> x6, waiting for transfers between devices: none -> 159 us  [collect(): theirs = lax.ppermute(grown, axis, [(d, d ^ reach) for d in range(ways)])]
    all_gather x3 -> x0, waiting for transfers between devices: 128 us -> none  [to_owners(): lax.all_gather(local_rows, 'head', axis=0, tiled=True)]
    ppermute x0 -> x6, starting transfers between devices: none -> 14.9 us  [collect(): theirs = lax.ppermute(grown, axis, [(d, d ^ reach) for d in range(ways)])]
    ppermute x2, starting transfers between devices: 6.22 us -> 17.3 us  [passed_along(): return lax.ppermute(array, axis, pairs)]
  transfers between devices with their start and end apart: 9 -> 12, of which waited for: 6 -> 9; matrix products, arithmetic and copies ran while one was open for 12% -> 10% of each run, Pallas kernels for 0% -> 0%
where the time goes in v1:
time: 599 us; the launch traced here: 590 us
  waiting for transfers between devices  332 us (55%)
  other arithmetic  61.7 us (10%)
  matrix products  58.2 us (10%)
  blocking collectives  48.2 us (8%)
  local copies, waits for them, and re-layouts  41.6 us (7%)
  starting transfers between devices  32.5 us (5%)
  between operations  14.7 us (2%)
    reduce_scatter x2, waiting for transfers between devices, from_owners(): lax.psum_scatter(term(jnp.int32(0), share_rows * lax.axis_size('head')),...  167 us
    ppermute x6, waiting for transfers between devices, collect(): theirs = lax.ppermute(grown, axis, [(d, d ^ reach) for d in range(ways)])  159 us
    pmax x1, blocking collectives, local(): logit_full, norm_full = lax.pmax((logit_full, norm_full), ('seq', 'head'))  39.1 us
    convert_element_type x6, local copies, waits for them, and re-layouts, unit_rows(): widened = values.astype(jnp.float32)  17.8 us
    ppermute x2, starting transfers between devices, passed_along(): return lax.ppermute(array, axis, pairs)  17.3 us
    add x16, other arithmetic, advance(): next_moment = moment_rate[:, None, None] * moment + current_written  16 us
    ppermute x6, starting transfers between devices, collect(): theirs = lax.ppermute(grown, axis, [(d, d ^ reach) for d in range(ways)])  14.9 us
    dot_general x1, matrix products, vocab_maxima(): jnp.dot(piece, vocab_weight, preferred_element_type=jnp.float32)  13.7 us
  transfers between devices with their start and end apart: 12, of which 9 were waited for; matrix products, arithmetic and copies ran while one was open for 10% of the time, Pallas kernels for 0%

profile of v1, /device:TPU:0, one launch (start us, length us, event | category | flops | bytes accessed | tf_op | source)
XLA Modules:
  0.0 589.7 jit_solution(3310690721261420830)
XLA Ops:
  7.3 3.1 collective-permute-start
  12.6 9.9 %collective-permute-done = bf16[256,1024]{1,0:T(8,128)(2,1)S(1)} collective-permute-done((bf16[256,1024]{1,0:T(8,128)(2,1)}, bf16[256,1024]{1,0:T(8,128)(2,1)S(1)}, u32[]{:S(2)}, u32[]{:S(2)}) %collective-permute-start) | collective-permute-done | bytes 524320 | tf_op jit(solution)/shard_map/ppermute | solution.py:22
  32.6 40.5 %collective-permute-done.1 = bf16[512,1024]{1,0:T(8,128)(2,1)} collective-permute-done((bf16[512,1024]{1,0:T(8,128)(2,1)}, bf16[512,1024]{1,0:T(8,128)(2,1)}, u32[]{:S(2)}, u32[]{:S(2)}) %collective-permute-start.1) | collective-permute-done | bytes 1048608 | tf_op jit(solution)/shard_map/ppermute | solution.py:22
  76.1 4.1 fusion.36
  89.0 3.5 copy.206
  92.5 3.1 convert_multiply_fusion.2
  95.6 3.5 fusion.57
  99.1 29.3 %while.34 = (s32[]{:T(128)}, f32[2,3]{0,1:T(4,128)S(1)}, f32[2,128,128]{2,1,0:T(8,128)S(1)}, f32[2,128,128]{2,1,0:T(8,128)S(1)}, f32[16,2,3]{2,1,0:T(2,128)S(1)}...) while((s32[]{:T(128)}, f32[2,3]{0,1:T(4,128)S(1)}, ...), condition=%wide.region_12.13_spmd.clone, body=%wide.region_11.12_spmd.clone.sunk | while | flops 262167 | bytes 919908 | solution.py:221
  130.4 6.4 %and_and_fusion = pred[1024,2048]{1,0:T(8,128)(4,1)} fusion(s32[2048]{0:T(1024)S(1)} %iota_add_fusion, s32[2048]{0:T(1024)S(1)} %fusion.72, s32[1024]{0:T(1024)S(1)} %iota_add_fusion.1, s32[1024]{0:T(1024)S(1)} %fusion.79, pred[2048]{0:T(1024)(128)(4,1)S(1)} %fusion.76), kind=kLoop, calls=%fused_computation.25 | loop fusion | flops 8388608 | bytes 2123776 | tf_op jit(solution)/shard_map/and | solution.py:155
  136.9 13.1 %collective-permute-start.2 = (bf16[1024,2,128]{0,2,1:T(8,128)(2,1)}, bf16[1024,2,128]{0,2,1:T(8,128)(2,1)}, u32[]{:S(2)}, u32[]{:S(2)}) collective-permute-start(bf16[1024,2,128]{0,2,1:T(8,128)(2,1)} %bitcast.5), channel_id=1, source_target_pairs={{0,4},{4,8},{8,12},{12,16},{16,20},{20,24},{24,28},{1,5},{5,9},{9,... | collective-permute-start | bytes 1572872 | tf_op jit(solution)/shard_map/ppermute | solution.py:33
  156.6 4.2 collective-permute-start.3
  160.9 9.1 %all-gather.3 = f32[8,2,3]{2,1,0:T(2,128)} all-gather(f32[1,2,3]{2,1,0:T(2,128)S(1)} %bitcast.114), channel_id=2, replica_groups=mesh['seq'=8,'head'=4] {'seq'}, dimensions={0}, use_global_device_ids=true | all-gather | bytes 216 | tf_op jit(solution)/shard_map/all_gather | solution.py:38
  173.0 3.5 copy.203
  180.1 3.3 fusion.45
  183.4 4.9 fusion.3
  188.4 5.6 fusion.4
  195.4 6.4 %all-gather.7.cloned.1.call-done = f32[16,128,128]{2,1,0:T(8,128)} async-done(((f32[2,128,128]{2,1,0:T(8,128)}), f32[16,128,128]{2,1,0:T(8,128)}) %all-gather.7.cloned.1.call-update) | async-done | bytes 1048592 | tf_op jit(solution)/shard_map/all_gather | solution.py:38
  202.6 4.3 fusion.42
  211.2 10.5 %fusion.49 = bf16[1024,2,128]{0,2,1:T(8,128)(2,1)S(1)} fusion(f32[1024,2,128]{0,2,1:T(8,128)} %copy.219, f32[1024,2,128]{0,2,1:T(8,128)} %convolution_bitcast_fusion, f32[2,1024,2048]{2,1,0:T(8,128)} %copy-done.5, f32[2,1024]{1,0:T(2,128)S(1)} %add.226, f32[2,1024]{1,0:T(2,128)S(1)} %max.11, pred[1024,2048]{1,0:T(8,128)(4,1)} %and_and_fusion, ...), kind=kOutput, calls=%fused_computation.75 | convolution fusion | flops 1101791232 | bytes 22560768 | tf_op jit(solution)/shard_map/hqk,khd->qhd/dot_general | solution.py:174
  224.7 89.8 %reduce-scatter.3.cloned.1.call-done = f32[256,1024]{1,0:T(8,128)} async-done(((f32[1024,1024]{1,0:T(8,128)}), f32[256,1024]{1,0:T(8,128)}) %reduce-scatter.3.cloned.1.call-update) | async-done | bytes 1048592 | tf_op jit(solution)/shard_map/reduce_scatter | solution.py:94
  317.8 12.2 %collective-permute-done.4 = bf16[256,1024]{1,0:T(8,128)(2,1)S(1)} collective-permute-done((bf16[256,1024]{1,0:T(8,128)(2,1)S(1)}, bf16[256,1024]{1,0:T(8,128)(2,1)S(1)}, u32[]{:S(2)}, u32[]{:S(2)}) %collective-permute-start.4) | collective-permute-done | bytes 524320 | tf_op jit(solution)/shard_map/ppermute | solution.py:22
  330.5 3.0 collective-permute-start.5
  333.5 44.8 %collective-permute-done.5 = bf16[512,1024]{1,0:T(8,128)(2,1)S(1)} collective-permute-done((bf16[512,1024]{1,0:T(8,128)(2,1)S(1)}, bf16[512,1024]{1,0:T(8,128)(2,1)S(1)}, u32[]{:S(2)}, u32[]{:S(2)}) %collective-permute-start.5) | collective-permute-done | bytes 1048608 | tf_op jit(solution)/shard_map/ppermute | solution.py:22
  378.3 3.5 fusion.12
  381.8 3.8 fusion.39
  385.7 76.9 %reduce-scatter.5.cloned.1.call-done = f32[256,1024]{1,0:T(8,128)} async-done(((f32[1024,1024]{1,0:T(8,128)}), f32[256,1024]{1,0:T(8,128)}) %reduce-scatter.5.cloned.1.call-update) | async-done | bytes 1048592 | tf_op jit(solution)/shard_map/reduce_scatter | solution.py:94
  466.6 12.2 %collective-permute-done.6 = bf16[256,1024]{1,0:T(8,128)(2,1)S(1)} collective-permute-done((bf16[256,1024]{1,0:T(8,128)(2,1)S(1)}, bf16[256,1024]{1,0:T(8,128)(2,1)S(1)}, u32[]{:S(2)}, u32[]{:S(2)}) %collective-permute-start.6) | collective-permute-done | bytes 524320 | tf_op jit(solution)/shard_map/ppermute | solution.py:22
  480.3 3.0 collective-permute-start.7
  483.6 3.0 slice.90
  489.3 39.2 %collective-permute-done.7 = bf16[512,1024]{1,0:T(8,128)(2,1)} collective-permute-done((bf16[512,1024]{1,0:T(8,128)(2,1)}, bf16[512,1024]{1,0:T(8,128)(2,1)}, u32[]{:S(2)}, u32[]{:S(2)}) %collective-permute-start.7) | collective-permute-done | bytes 1048608 | tf_op jit(solution)/shard_map/ppermute | solution.py:22
  528.4 13.7 %convolution_reduce_fusion = f32[1024]{0:T(1024)S(1)} fusion(bf16[1024,4096]{1,0:T(8,128)(2,1)} %param.22, bf16[512,1024]{1,0:T(8,128)(2,1)} %collective-permute-done.7, bf16[512,1024]{1,0:T(8,128)(2,1)} %maximum_select_fusion.7, pred[]{:T(512)S(6)} %eq.57), kind=kOutput, calls=%fused_computation.32 | convolution fusion | flops 8603565056 | bytes 10489857 | tf_op jit(solution)/shard_map/dot_general | solution.py:279
  542.5 39.1 %all-reduce = (f32[8192]{0:T(1024)S(1)}, f32[4,8]{0,1:T(8,128)S(1)}) all-reduce(f32[8192]{0:T(1024)S(1)} %dynamic_update_slice.14, f32[4,8]{0,1:T(8,128)S(1)} %constant_dynamic-update-slice_fusion.1), channel_id=1, replica_groups=mesh['seq'=8,'head'=4] {'seq','head'}, use_global_device_ids=true, to_apply=%region_20.21 | all-reduce | flops 8224 | bytes 65792 | tf_op jit(solution)/shard_map/pmax | solution.py:291
  (294 shorter events, 91.1 us)
Async XLA Ops:
  7.2 371.2 %copy-start = (bf16[1024,2,704]{0,2,1:T(8,128)(2,1)S(1)}, bf16[1024,2,704]{0,2,1:T(8,128)(2,1)}, u32[]{:S(2)}) copy-start(bf16[1024,2,704]{0,2,1:T(8,128)(2,1)} %param.20) | copy-start | bytes 8650756
  7.2 20.7 %copy-start.32 = (f32[16,2]{0,1:T(2,128)S(1)}, f32[16,2]{0,1:T(2,128)}, u32[]{:S(2)}) copy-start(f32[16,2]{0,1:T(2,128)} %param.26) | copy-start | bytes 388
  7.2 20.8 %copy-start.33 = (f32[16,2]{0,1:T(2,128)S(1)}, f32[16,2]{0,1:T(2,128)}, u32[]{:S(2)}) copy-start(f32[16,2]{0,1:T(2,128)} %param.27) | copy-start | bytes 388
  7.2 20.9 %copy-start.29 = (f32[1024,2]{0,1:T(2,128)S(1)}, f32[1024,2]{0,1:T(2,128)}, u32[]{:S(2)}) copy-start(f32[1024,2]{0,1:T(2,128)} %param.25) | copy-start | bytes 24580
  7.2 188.2 %all-gather.9.cloned.1.call-start = ((), (), s32[]{:S(2)}) async-start(), calls=%async_computation.5 | async-start | bytes 1179648 | tf_op jit(solution)/shard_map/all_gather | solution.py:38
  7.3 15.2 %collective-permute-start = (bf16[256,1024]{1,0:T(8,128)(2,1)}, bf16[256,1024]{1,0:T(8,128)(2,1)S(1)}, u32[]{:S(2)}, u32[]{:S(2)}) collective-permute-start(bf16[256,1024]{1,0:T(8,128)(2,1)} %param.17), channel_id=1, source_target_pairs={{0,1},{1,0},{2,3},{3,2},{4,5},{5,4},{6,7},{7,6},{8,9},{9,8},{10,11... | collective-permute-start | bytes 1572872 | tf_op jit(solution)/shard_map/ppermute | solution.py:22
  11.2 11.3 %copy-start.37 = (s32[16]{0:T(128)}, s32[16]{0:T(128)S(1)}, u32[]{:S(2)}) copy-start(s32[16]{0:T(128)S(1)} %iota_add_fusion.2) | copy-start | bytes 196
  25.1 6.8 %copy-start.25 = (bf16[2,16,256]{2,1,0:T(8,128)(2,1)S(1)}, bf16[2,16,256]{2,1,0:T(8,128)(2,1)}, u32[]{:S(2)}) copy-start(bf16[2,16,256]{2,1,0:T(8,128)(2,1)} %param.23) | copy-start | bytes 49156
  25.1 6.8 %copy-start.26 = (f32[3,1024]{1,0:T(4,128)S(1)}, f32[3,1024]{1,0:T(4,128)}, u32[]{:S(2)}) copy-start(f32[3,1024]{1,0:T(4,128)} %param.24) | copy-start | bytes 36868
  25.1 48.0 %collective-permute-start.1 = (bf16[512,1024]{1,0:T(8,128)(2,1)}, bf16[512,1024]{1,0:T(8,128)(2,1)}, u32[]{:S(2)}, u32[]{:S(2)}) collective-permute-start(bf16[512,1024]{1,0:T(8,128)(2,1)} %maximum_select_fusion.5), channel_id=1, source_target_pairs={{0,2},{1,3},{2,0},{3,1},{4,6},{5,7},{6,4},{7,5},{8,10},{9,11},{10,... | collective-permute-start | bytes 3145736 | tf_op jit(solution)/shard_map/ppermute | solution.py:22
  31.8 44.3 %copy-start.16 = (bf16[1024,3,256]{0,2,1:T(8,128)(2,1)S(1)}, bf16[1024,3,256]{0,2,1:T(8,128)(2,1)}, u32[]{:S(2)}) copy-start(bf16[1024,3,256]{0,2,1:T(8,128)(2,1)} %copy.195) | copy-start | bytes 4718596
  128.4 24.1 %copy-start.1 = (f32[2,128,128]{2,1,0:T(8,128)}, f32[2,128,128]{2,1,0:T(8,128)S(1)}, u32[]{:S(2)}) copy-start(f32[2,128,128]{2,1,0:T(8,128)S(1)} %get-tuple-element.115) | copy-start | bytes 393220
  128.4 48.0 %copy-start.18 = (f32[16,2,3]{2,1,0:T(2,128)}, f32[16,2,3]{2,1,0:T(2,128)S(1)}, u32[]{:S(2)}) copy-start(f32[16,2,3]{2,1,0:T(2,128)S(1)} %get-tuple-element.113) | copy-start | bytes 1156
  129.1 72.7 %all-gather.7.cloned.1.call-start = ((), (), s32[]{:S(2)}) async-start(), calls=%async_computation.4 | async-start | bytes 1179648 | tf_op jit(solution)/shard_map/all_gather | solution.py:38
  136.9 74.4 %collective-permute-start.2 = (bf16[1024,2,128]{0,2,1:T(8,128)(2,1)}, bf16[1024,2,128]{0,2,1:T(8,128)(2,1)}, u32[]{:S(2)}, u32[]{:S(2)}) collective-permute-start(bf16[1024,2,128]{0,2,1:T(8,128)(2,1)} %bitcast.5), channel_id=1, source_target_pairs={{0,4},{4,8},{8,12},{12,16},{16,20},{20,24},{24,28},{1,5},{5,9},{9,... | collective-permute-start | bytes 1572872 | tf_op jit(solution)/shard_map/ppermute | solution.py:33
  156.6 26.7 %collective-permute-start.3 = (bf16[1024,2,128]{2,0,1:T(8,128)(2,1)S(1)}, bf16[1024,2,128]{2,0,1:T(8,128)(2,1)}, u32[]{:S(2)}, u32[]{:S(2)}) collective-permute-start(bf16[1024,2,128]{2,0,1:T(8,128)(2,1)S(1)} %multiply_convert_fusion.4), channel_id=1, source_target_pairs={{0,4},{4,8},{8,12},{12,16},{16,20},{20,24},{24,28},{1,5},{5,9},{9,... | collective-permute-start | bytes 1572872 | tf_op jit(solution)/shard_map/ppermute | solution.py:33
  160.9 11.9 %copy-start.27 = (f32[2,3]{1,0:T(2,128)}, f32[2,3]{1,0:T(2,128)S(1)}, u32[]{:S(2)}) copy-start(f32[2,3]{1,0:T(2,128)S(1)} %copy.215) | copy-start | bytes 76
  178.1 136.3 %reduce-scatter.3.cloned.1.call-start = ((), (), s32[]{:S(2)}) async-start(), calls=%async_computation.2 | async-start | bytes 5242880 | tf_op jit(solution)/shard_map/reduce_scatter | solution.py:94
  211.2 10.5 %copy-start.17 = (bf16[256,1024]{1,0:T(8,128)(2,1)S(1)}, bf16[256,1024]{1,0:T(8,128)(2,1)}, u32[]{:S(2)}) copy-start(bf16[256,1024]{1,0:T(8,128)(2,1)} %param.19) | copy-start | bytes 1572868
  224.4 90.1 %copy-start.6 = (bf16[256,1024]{1,0:T(8,128)(2,1)S(1)}, bf16[256,1024]{1,0:T(8,128)(2,1)}, u32[]{:S(2)}) copy-start(bf16[256,1024]{1,0:T(8,128)(2,1)} %param.17) | copy-start | bytes 1572868
  224.4 91.6 %copy-start.24 = (f32[1,1024]{1,0:T(1,128)S(1)}, f32[1,1024]{1,0:T(1,128)}, u32[]{:S(2)}) copy-start(f32[1,1024]{1,0:T(1,128)} %get-tuple-element.208) | copy-start | bytes 12292
  224.4 238.2 %reduce-scatter.5.cloned.1.call-start = ((), (), s32[]{:S(2)}) async-start(), calls=%async_computation.3 | async-start | bytes 5242880 | tf_op jit(solution)/shard_map/reduce_scatter | solution.py:94
  316.2 13.7 %collective-permute-start.4 = (bf16[256,1024]{1,0:T(8,128)(2,1)S(1)}, bf16[256,1024]{1,0:T(8,128)(2,1)S(1)}, u32[]{:S(2)}, u32[]{:S(2)}) collective-permute-start(bf16[256,1024]{1,0:T(8,128)(2,1)S(1)} %multiply_convert_fusion.1), channel_id=1, source_target_pairs={{0,1},{1,0},{2,3},{3,2},{4,5},{5,4},{6,7},{7,6},{8,9},{9,8},{10,11... | collective-permute-start | bytes 1572872 | tf_op jit(solution)/shard_map/ppermute | solution.py:22
  330.5 47.9 %collective-permute-start.5 = (bf16[512,1024]{1,0:T(8,128)(2,1)S(1)}, bf16[512,1024]{1,0:T(8,128)(2,1)S(1)}, u32[]{:S(2)}, u32[]{:S(2)}) collective-permute-start(bf16[512,1024]{1,0:T(8,128)(2,1)S(1)} %maximum_select_fusion.6), channel_id=1, source_target_pairs={{0,2},{1,3},{2,0},{3,1},{4,6},{5,7},{6,4},{7,5},{8,10},{9,11},{10,... | collective-permute-start | bytes 3145736 | tf_op jit(solution)/shard_map/ppermute | solution.py:22
  464.8 18.7 %copy-start.19 = (f32[16,2,3]{2,1,0:T(2,128)S(1)}, f32[16,2,3]{2,1,0:T(2,128)}, u32[]{:S(2)}) copy-start(f32[16,2,3]{2,1,0:T(2,128)} %copy-done.18) | copy-start | bytes 1156
  465.0 18.3 %copy-start.34 = (s32[4]{0:T(128)S(1)}, s32[4]{0:T(128)}, u32[]{:S(2)}) copy-start(s32[4]{0:T(128)} %get-tuple-element.211) | copy-start | bytes 52
  465.0 18.3 %copy-start.38 = (s32[16]{0:T(128)S(1)}, s32[16]{0:T(128)}, u32[]{:S(2)}) copy-start(s32[16]{0:T(128)} %copy-done.37) | copy-start | bytes 196
  465.1 18.3 %copy-start.28 = (f32[2,3]{1,0:T(2,128)S(1)}, f32[2,3]{1,0:T(2,128)}, u32[]{:S(2)}) copy-start(f32[2,3]{1,0:T(2,128)} %copy-done.27) | copy-start | bytes 76
  465.1 13.8 %collective-permute-start.6 = (bf16[256,1024]{1,0:T(8,128)(2,1)S(1)}, bf16[256,1024]{1,0:T(8,128)(2,1)S(1)}, u32[]{:S(2)}, u32[]{:S(2)}) collective-permute-start(bf16[256,1024]{1,0:T(8,128)(2,1)S(1)} %multiply_convert_fusion), channel_id=1, source_target_pairs={{0,1},{1,0},{2,3},{3,2},{4,5},{5,4},{6,7},{7,6},{8,9},{9,8},{10,11... | collective-permute-start | bytes 1572872 | tf_op jit(solution)/shard_map/ppermute | solution.py:22
  480.3 6.6 %copy-start.2 = (f32[2,128,128]{2,1,0:T(8,128)S(1)}, f32[2,128,128]{2,1,0:T(8,128)}, u32[]{:S(2)}) copy-start(f32[2,128,128]{2,1,0:T(8,128)} %copy-done.1) | copy-start | bytes 393220
  480.3 6.6 %copy-start.9 = (f32[2,128,128]{2,1,0:T(8,128)S(1)}, f32[2,128,128]{2,1,0:T(8,128)}, u32[]{:S(2)}) copy-start(f32[2,128,128]{2,1,0:T(8,128)} %copy-done.8) | copy-start | bytes 393220
  480.3 48.1 %collective-permute-start.7 = (bf16[512,1024]{1,0:T(8,128)(2,1)}, bf16[512,1024]{1,0:T(8,128)(2,1)}, u32[]{:S(2)}, u32[]{:S(2)}) collective-permute-start(bf16[512,1024]{1,0:T(8,128)(2,1)} %maximum_select_fusion.7), channel_id=1, source_target_pairs={{0,2},{1,3},{2,0},{3,1},{4,6},{5,7},{6,4},{7,5},{8,10},{9,11},{10,... | collective-permute-start | bytes 3145736 | tf_op jit(solution)/shard_map/ppermute | solution.py:22
  (19 other events, 56.8 us)
Sparse Core Ops, SparseCore 0:
  129.2 24.4 all-gather.8
  178.2 23.5 all-gather.6
  224.6 89.8 reduce-scatter.2
  385.8 76.7 reduce-scatter.4
